TPU v7x, 32 devices: a whole 2x2x4 slice. The times are simulated.
32 devices in a mesh: parts: 2 (over x), rows: 2 (over core), cols: 8 (over z, y).
Axes of the slice: x: 2, y: 2, z: 4, core: 2. Of those that a mesh axis runs over, the one named last changes fastest.
Arguments:
- src_feat: float32 [32, 131072], P(None, ('parts', 'rows', 'cols')), parts along dimension 1, may hold values from -0.75 to 0.75
- tgt_feat: float32 [32, 16384], P(None, ('parts', 'cols')), parts along dimension 1, may hold values from -0.75 to 0.75
- tgt_pot: float32 [16384], P(('parts', 'cols')), parts along dimension 0, may hold values from -25 to 25
- log_src: float32 [131072], P(('parts', 'rows', 'cols')), parts along dimension 0, may hold values from -3 to 3
- log_tgt: float32 [16384], P(('parts', 'cols')), parts along dimension 0, may hold values from -3 to 3
- pairs: int32 [512, 24], P(('parts', 'rows', 'cols')), parts along dimension 0, may hold values from 0 to 31, as said below
- counts: int32 [512], P(('parts', 'rows', 'cols')), parts along dimension 0, may hold values from 1 to 24, as said below
Outputs:
- src_pot: float32 [131072], P(('parts', 'rows', 'cols')), parts along dimension 0
- new_tgt_pot: float32 [16384], P(('parts', 'cols')), parts along dimension 0
There are 2 independent parts, one for each index of `parts`. A program takes and returns all parts, laid end to end along the dimension named above; each array names one. Nothing has to cross between parts.
Inputs may be any that keep to these rules, and one draw needn't show every extreme that they name: `pairs`: each row names 24 different target blocks, and every target block is the first entry of some row. `counts`: row 0 uses all 24 entries and row 1 only one.
All inputs are finite; a program needn't handle non-finite values.
Results may differ from a plain program's by a relative error of at most 0.0003.
Values sent between devices are 32-bit elements; how exact they have to be, the bound alone decides.
No kernel may reach another device: no remote copies, remote signals or barrier semaphores. Data moves between devices by JAX's collectives and lax.ppermute only.
A program may use at most 128 MiB of HBM per device.

v0:
```python
import jax
import jax.numpy as jnp
from jax import lax
from jax.sharding import PartitionSpec as P

D = 32
BLK = 256
GROUP = 8
epsilon = 0.1
NEG = -1e30


def joined(array, axis, combine):
    everything = jax.tree.map(lambda part: lax.all_gather(part, axis), array)
    initial = jax.tree.map(lambda part: part[0], everything)

    def step(k, so_far):
        return combine(so_far, jax.tree.map(lambda part: part[k], everything))

    return lax.fori_loop(1, lax.axis_size(axis), step, initial)


def combine_parts(first, second):
    top = jnp.maximum(first[0], second[0])
    total = first[1] * jnp.exp(first[0] - top) + second[1] * jnp.exp(second[0] - top)
    return (top, total)


def on_device(src_feat, tgt_feat, tgt_pot, log_src, log_tgt, pairs, counts):
    own_targets = tgt_feat.shape[1]
    packed = jnp.concatenate([tgt_feat, tgt_pot[None, :], log_tgt[None, :]], axis=0)
    whole = lax.all_gather(packed, "cols", axis=1, tiled=True)
    feats = whole[:D]
    ynorm = jnp.sum(feats * feats, axis=0)
    tblocks = whole.shape[1] // BLK
    table = jnp.concatenate([whole, ynorm[None, :]], axis=0)
    blocks = jnp.transpose(table.reshape(D + 3, tblocks, BLK), (1, 0, 2))
    within = jnp.arange(GROUP, dtype=jnp.int32)
    block_numbers = jnp.arange(tblocks, dtype=jnp.int32)

    def row_step(carry, index):
        start = index * BLK
        xs = lax.dynamic_slice_in_dim(src_feat, start, BLK, 1)
        weights = lax.dynamic_slice_in_dim(log_src, start, BLK, 0)
        xnorm = jnp.sum(xs * xs, axis=0)
        row_ids = pairs[index]
        count = counts[index]
        ngroups = (count + GROUP - 1) // GROUP
        slabs = jnp.take(blocks, row_ids, axis=0)

        def take_group(step):
            ids = lax.dynamic_slice_in_dim(row_ids, step * GROUP, GROUP, 0)
            group = lax.dynamic_slice_in_dim(slabs, step * GROUP, GROUP, 0)
            mask = jnp.repeat(step * GROUP + within < count, BLK)
            cross = jnp.einsum(
                "dr,gdc->rgc",
                xs,
                group[:, :D, :],
                precision=lax.Precision.HIGHEST,
                preferred_element_type=jnp.float32,
            ).reshape(BLK, GROUP * BLK)
            cost = xnorm[:, None] + group[:, D + 2, :].reshape(-1)[None, :] - 2.0 * cross
            return (ids, mask, group, cost)

        def row_pass(step, state):
            run_top, run_sum = state
            ids, mask, group, cost = take_group(step)
            pots = group[:, D, :].reshape(-1)
            logs = group[:, D + 1, :].reshape(-1)
            scores = jnp.where(mask[None, :], logs[None, :] + (pots[None, :] - cost) / epsilon, NEG)
            top = jnp.maximum(run_top, jnp.max(scores, axis=1))
            run_sum = run_sum * jnp.exp(run_top - top) + jnp.sum(
                jnp.exp(scores - top[:, None]), axis=1
            )
            return (top, run_sum)

        start_state = (jnp.full((BLK,), NEG, jnp.float32), jnp.zeros((BLK,), jnp.float32))
        run_top, run_sum = lax.fori_loop(0, ngroups, row_pass, start_state)
        fpot = -epsilon * (run_top + jnp.log(run_sum))

        def col_pass(step, state):
            acc_top, acc_sum = state
            ids, mask, group, cost = take_group(step)
            scores = jnp.where(
                mask[None, :], weights[:, None] + (fpot[:, None] - cost) / epsilon, NEG
            )
            col_top = jnp.max(scores, axis=0)
            col_sum = jnp.where(mask, jnp.sum(jnp.exp(scores - col_top[None, :]), axis=0), 0.0)
            col_top = col_top.reshape(GROUP, BLK)
            col_sum = col_sum.reshape(GROUP, BLK)
            selector = ids[:, None] == block_numbers[None, :]
            onehot = selector.astype(jnp.float32)
            landed = jnp.max(jnp.where(selector[:, :, None], col_top[:, None, :], NEG), axis=0)
            top = jnp.maximum(acc_top, landed)
            top_here = jnp.einsum(
                "gt,tb->gb",
                onehot,
                top,
                precision=lax.Precision.HIGHEST,
                preferred_element_type=jnp.float32,
            )
            added = jnp.einsum(
                "gt,gb->tb",
                onehot,
                col_sum * jnp.exp(col_top - top_here),
                precision=lax.Precision.HIGHEST,
                preferred_element_type=jnp.float32,
            )
            fresh = acc_sum * jnp.exp(acc_top - top) + added
            return (top, fresh)

        carry = lax.fori_loop(0, ngroups, col_pass, carry)
        return (carry, fpot)

    init = (jnp.full((tblocks, BLK), NEG, jnp.float32), jnp.zeros((tblocks, BLK), jnp.float32))
    (acc_top, acc_sum), fblocks = lax.scan(
        row_step, init, jnp.arange(pairs.shape[0], dtype=jnp.int32)
    )
    src_pot = fblocks.reshape(-1)
    flat_top = acc_top.reshape(-1)
    flat_sum = acc_sum.reshape(-1)
    owner_start = lax.axis_index("cols") * own_targets
    all_top, all_sum = joined((flat_top, flat_sum), ("rows", "cols"), combine_parts)
    own_top = lax.dynamic_slice_in_dim(all_top, owner_start, own_targets, 0)
    own_sum = lax.dynamic_slice_in_dim(all_sum, owner_start, own_targets, 0)
    new_tgt_pot = -epsilon * (own_top + jnp.log(own_sum))
    return (src_pot, new_tgt_pot)


def solution(mesh):
    placed = (
        P(None, ("parts", "rows", "cols")),
        P(None, ("parts", "cols")),
        P(("parts", "cols")),
        P(("parts", "rows", "cols")),
        P(("parts", "cols")),
        P(("parts", "rows", "cols"), None),
        P(("parts", "rows", "cols")),
    )
    return jax.shard_map(
        on_device,
        mesh=mesh,
        in_specs=placed,
        out_specs=(P(("parts", "rows", "cols")), P(("parts", "cols"))),
        check_vma=False,
    )
```

profile of v0, /device:TPU:0, one launch (start us, length us, event | category | flops | bytes accessed | tf_op | source)
XLA Modules:
  0.0 660.8 jit_solution(5542897578245292571)
XLA Ops:
  8.9 46.1 %all-gather.4.cloned.1.call-done = f32[34,8192]{1,0:T(8,128)} async-done(((f32[34,1024]{1,0:T(8,128)}), f32[34,8192]{1,0:T(8,128)}) %all-gather.4.cloned.1.call-update) | async-done | bytes 1114128 | tf_op jit(solution)/shard_map/all_gather | solution.py:32
  57.9 446.4 %while.113 = (s32[]{:T(128)}, f32[32,256]{1,0:T(8,128)S(1)}, f32[32,256]{1,0:T(8,128)S(1)}, f32[16,256]{1,0:T(8,128)S(1)}, s32[16]{0:T(128)S(1)}, /*index=5*/s32...) while((s32[]{:T(128)}, f32[32,256]{1,0:T(8,128)S(1)}, ...), condition=%wide.region_12.13_spmd.clone.clone, body=%wide.region_1.12_spmd.clone.clone.sunk | while | flops 415103776 | bytes 13110493 | solution.py:116
  65.5 12.1 %while.114 = (s32[]{:T(128)}, f32[256]{0:T(256)S(1)}, f32[256]{0:T(256)S(1)}, s32[]{:T(128)}, s32[8]{0:T(128)S(1)}, /*index=5*/s32[]{:T(128)}, f32[24,35,256]{2,...) while((s32[]{:T(128)}, f32[256]{0:T(256)S(1)}, ...), condition=%wide.region_6.6_spmd, body=%wide.region_3.5_spmd.sunk | while | flops 206570016 | bytes 4627243 | solution.py:78
  66.3 2.9 fusion.43
  70.3 2.9 fusion.43
  74.4 2.9 fusion.43
  78.4 12.5 %while.115 = (s32[]{:T(128)}, f32[32,256]{1,0:T(8,128)S(1)}, f32[32,256]{1,0:T(8,128)S(1)}, s32[]{:T(128)}, s32[24]{0:T(128)S(1)}, /*index=5*/s32[32]{0:T(128)S(...) while((s32[]{:T(128)}, f32[32,256]{1,0:T(8,128)S(1)}, ...), condition=%wide.region_11.11_spmd, body=%wide.region_7.10_spmd.sunk | while | flops 208300816 | bytes 4961095 | solution.py:112
  98.5 4.1 while.114
  103.4 4.1 while.115
  115.1 12.1 %while.114 = (s32[]{:T(128)}, f32[256]{0:T(256)S(1)}, f32[256]{0:T(256)S(1)}, s32[]{:T(128)}, s32[8]{0:T(128)S(1)}, /*index=5*/s32[]{:T(128)}, f32[24,35,256]{2,...) while((s32[]{:T(128)}, f32[256]{0:T(256)S(1)}, ...), condition=%wide.region_6.6_spmd, body=%wide.region_3.5_spmd.sunk | while | flops 206570016 | bytes 4627243 | solution.py:78
  119.9 2.9 fusion.43
  124.0 2.9 fusion.43
  128.0 12.5 %while.115 = (s32[]{:T(128)}, f32[32,256]{1,0:T(8,128)S(1)}, f32[32,256]{1,0:T(8,128)S(1)}, s32[]{:T(128)}, s32[24]{0:T(128)S(1)}, /*index=5*/s32[32]{0:T(128)S(...) while((s32[]{:T(128)}, f32[32,256]{1,0:T(8,128)S(1)}, ...), condition=%wide.region_11.11_spmd, body=%wide.region_7.10_spmd.sunk | while | flops 208300816 | bytes 4961095 | solution.py:112
  148.1 8.1 %while.114 = (s32[]{:T(128)}, f32[256]{0:T(256)S(1)}, f32[256]{0:T(256)S(1)}, s32[]{:T(128)}, s32[8]{0:T(128)S(1)}, /*index=5*/s32[]{:T(128)}, f32[24,35,256]{2,...) while((s32[]{:T(128)}, f32[256]{0:T(256)S(1)}, ...), condition=%wide.region_6.6_spmd, body=%wide.region_3.5_spmd.sunk | while | flops 206570016 | bytes 4627243 | solution.py:78
  157.0 8.3 %while.115 = (s32[]{:T(128)}, f32[32,256]{1,0:T(8,128)S(1)}, f32[32,256]{1,0:T(8,128)S(1)}, s32[]{:T(128)}, s32[24]{0:T(128)S(1)}, /*index=5*/s32[32]{0:T(128)S(...) while((s32[]{:T(128)}, f32[32,256]{1,0:T(8,128)S(1)}, ...), condition=%wide.region_11.11_spmd, body=%wide.region_7.10_spmd.sunk | while | flops 208300816 | bytes 4961095 | solution.py:112
  173.0 12.1 %while.114 = (s32[]{:T(128)}, f32[256]{0:T(256)S(1)}, f32[256]{0:T(256)S(1)}, s32[]{:T(128)}, s32[8]{0:T(128)S(1)}, /*index=5*/s32[]{:T(128)}, f32[24,35,256]{2,...) while((s32[]{:T(128)}, f32[256]{0:T(256)S(1)}, ...), condition=%wide.region_6.6_spmd, body=%wide.region_3.5_spmd.sunk | while | flops 206570016 | bytes 4627243 | solution.py:78
  173.7 2.9 fusion.43
  177.8 2.9 fusion.43
  185.9 12.5 %while.115 = (s32[]{:T(128)}, f32[32,256]{1,0:T(8,128)S(1)}, f32[32,256]{1,0:T(8,128)S(1)}, s32[]{:T(128)}, s32[24]{0:T(128)S(1)}, /*index=5*/s32[32]{0:T(128)S(...) while((s32[]{:T(128)}, f32[32,256]{1,0:T(8,128)S(1)}, ...), condition=%wide.region_11.11_spmd, body=%wide.region_7.10_spmd.sunk | while | flops 208300816 | bytes 4961095 | solution.py:112
  206.0 12.1 %while.114 = (s32[]{:T(128)}, f32[256]{0:T(256)S(1)}, f32[256]{0:T(256)S(1)}, s32[]{:T(128)}, s32[8]{0:T(128)S(1)}, /*index=5*/s32[]{:T(128)}, f32[24,35,256]{2,...) while((s32[]{:T(128)}, f32[256]{0:T(256)S(1)}, ...), condition=%wide.region_6.6_spmd, body=%wide.region_3.5_spmd.sunk | while | flops 206570016 | bytes 4627243 | solution.py:78
  206.8 2.9 fusion.43
  214.9 2.9 fusion.43
  218.9 12.5 %while.115 = (s32[]{:T(128)}, f32[32,256]{1,0:T(8,128)S(1)}, f32[32,256]{1,0:T(8,128)S(1)}, s32[]{:T(128)}, s32[24]{0:T(128)S(1)}, /*index=5*/s32[32]{0:T(128)S(...) while((s32[]{:T(128)}, f32[32,256]{1,0:T(8,128)S(1)}, ...), condition=%wide.region_11.11_spmd, body=%wide.region_7.10_spmd.sunk | while | flops 208300816 | bytes 4961095 | solution.py:112
  239.0 8.1 %while.114 = (s32[]{:T(128)}, f32[256]{0:T(256)S(1)}, f32[256]{0:T(256)S(1)}, s32[]{:T(128)}, s32[8]{0:T(128)S(1)}, /*index=5*/s32[]{:T(128)}, f32[24,35,256]{2,...) while((s32[]{:T(128)}, f32[256]{0:T(256)S(1)}, ...), condition=%wide.region_6.6_spmd, body=%wide.region_3.5_spmd.sunk | while | flops 206570016 | bytes 4627243 | solution.py:78
  239.8 2.9 fusion.43
  247.9 8.3 %while.115 = (s32[]{:T(128)}, f32[32,256]{1,0:T(8,128)S(1)}, f32[32,256]{1,0:T(8,128)S(1)}, s32[]{:T(128)}, s32[24]{0:T(128)S(1)}, /*index=5*/s32[32]{0:T(128)S(...) while((s32[]{:T(128)}, f32[32,256]{1,0:T(8,128)S(1)}, ...), condition=%wide.region_11.11_spmd, body=%wide.region_7.10_spmd.sunk | while | flops 208300816 | bytes 4961095 | solution.py:112
  263.8 12.1 %while.114 = (s32[]{:T(128)}, f32[256]{0:T(256)S(1)}, f32[256]{0:T(256)S(1)}, s32[]{:T(128)}, s32[8]{0:T(128)S(1)}, /*index=5*/s32[]{:T(128)}, f32[24,35,256]{2,...) while((s32[]{:T(128)}, f32[256]{0:T(256)S(1)}, ...), condition=%wide.region_6.6_spmd, body=%wide.region_3.5_spmd.sunk | while | flops 206570016 | bytes 4627243 | solution.py:78
  264.6 2.9 fusion.43
  268.7 2.9 fusion.43
  272.7 2.9 fusion.43
  276.8 12.5 %while.115 = (s32[]{:T(128)}, f32[32,256]{1,0:T(8,128)S(1)}, f32[32,256]{1,0:T(8,128)S(1)}, s32[]{:T(128)}, s32[24]{0:T(128)S(1)}, /*index=5*/s32[32]{0:T(128)S(...) while((s32[]{:T(128)}, f32[32,256]{1,0:T(8,128)S(1)}, ...), condition=%wide.region_11.11_spmd, body=%wide.region_7.10_spmd.sunk | while | flops 208300816 | bytes 4961095 | solution.py:112
  296.9 8.1 %while.114 = (s32[]{:T(128)}, f32[256]{0:T(256)S(1)}, f32[256]{0:T(256)S(1)}, s32[]{:T(128)}, s32[8]{0:T(128)S(1)}, /*index=5*/s32[]{:T(128)}, f32[24,35,256]{2,...) while((s32[]{:T(128)}, f32[256]{0:T(256)S(1)}, ...), condition=%wide.region_6.6_spmd, body=%wide.region_3.5_spmd.sunk | while | flops 206570016 | bytes 4627243 | solution.py:78
  297.7 2.9 fusion.43
  305.8 8.3 %while.115 = (s32[]{:T(128)}, f32[32,256]{1,0:T(8,128)S(1)}, f32[32,256]{1,0:T(8,128)S(1)}, s32[]{:T(128)}, s32[24]{0:T(128)S(1)}, /*index=5*/s32[32]{0:T(128)S(...) while((s32[]{:T(128)}, f32[32,256]{1,0:T(8,128)S(1)}, ...), condition=%wide.region_11.11_spmd, body=%wide.region_7.10_spmd.sunk | while | flops 208300816 | bytes 4961095 | solution.py:112
  321.7 8.1 %while.114 = (s32[]{:T(128)}, f32[256]{0:T(256)S(1)}, f32[256]{0:T(256)S(1)}, s32[]{:T(128)}, s32[8]{0:T(128)S(1)}, /*index=5*/s32[]{:T(128)}, f32[24,35,256]{2,...) while((s32[]{:T(128)}, f32[256]{0:T(256)S(1)}, ...), condition=%wide.region_6.6_spmd, body=%wide.region_3.5_spmd.sunk | while | flops 206570016 | bytes 4627243 | solution.py:78
  322.5 2.9 fusion.43
  326.5 2.9 fusion.43
  330.6 8.3 %while.115 = (s32[]{:T(128)}, f32[32,256]{1,0:T(8,128)S(1)}, f32[32,256]{1,0:T(8,128)S(1)}, s32[]{:T(128)}, s32[24]{0:T(128)S(1)}, /*index=5*/s32[32]{0:T(128)S(...) while((s32[]{:T(128)}, f32[32,256]{1,0:T(8,128)S(1)}, ...), condition=%wide.region_11.11_spmd, body=%wide.region_7.10_spmd.sunk | while | flops 208300816 | bytes 4961095 | solution.py:112
  346.5 8.1 %while.114 = (s32[]{:T(128)}, f32[256]{0:T(256)S(1)}, f32[256]{0:T(256)S(1)}, s32[]{:T(128)}, s32[8]{0:T(128)S(1)}, /*index=5*/s32[]{:T(128)}, f32[24,35,256]{2,...) while((s32[]{:T(128)}, f32[256]{0:T(256)S(1)}, ...), condition=%wide.region_6.6_spmd, body=%wide.region_3.5_spmd.sunk | while | flops 206570016 | bytes 4627243 | solution.py:78
  347.3 2.9 fusion.43
  351.3 2.9 fusion.43
  355.4 8.3 %while.115 = (s32[]{:T(128)}, f32[32,256]{1,0:T(8,128)S(1)}, f32[32,256]{1,0:T(8,128)S(1)}, s32[]{:T(128)}, s32[24]{0:T(128)S(1)}, /*index=5*/s32[32]{0:T(128)S(...) while((s32[]{:T(128)}, f32[32,256]{1,0:T(8,128)S(1)}, ...), condition=%wide.region_11.11_spmd, body=%wide.region_7.10_spmd.sunk | while | flops 208300816 | bytes 4961095 | solution.py:112
  371.3 8.1 %while.114 = (s32[]{:T(128)}, f32[256]{0:T(256)S(1)}, f32[256]{0:T(256)S(1)}, s32[]{:T(128)}, s32[8]{0:T(128)S(1)}, /*index=5*/s32[]{:T(128)}, f32[24,35,256]{2,...) while((s32[]{:T(128)}, f32[256]{0:T(256)S(1)}, ...), condition=%wide.region_6.6_spmd, body=%wide.region_3.5_spmd.sunk | while | flops 206570016 | bytes 4627243 | solution.py:78
  372.1 2.9 fusion.43
  376.2 2.9 fusion.43
  380.2 8.3 %while.115 = (s32[]{:T(128)}, f32[32,256]{1,0:T(8,128)S(1)}, f32[32,256]{1,0:T(8,128)S(1)}, s32[]{:T(128)}, s32[24]{0:T(128)S(1)}, /*index=5*/s32[32]{0:T(128)S(...) while((s32[]{:T(128)}, f32[32,256]{1,0:T(8,128)S(1)}, ...), condition=%wide.region_11.11_spmd, body=%wide.region_7.10_spmd.sunk | while | flops 208300816 | bytes 4961095 | solution.py:112
  396.1 8.1 %while.114 = (s32[]{:T(128)}, f32[256]{0:T(256)S(1)}, f32[256]{0:T(256)S(1)}, s32[]{:T(128)}, s32[8]{0:T(128)S(1)}, /*index=5*/s32[]{:T(128)}, f32[24,35,256]{2,...) while((s32[]{:T(128)}, f32[256]{0:T(256)S(1)}, ...), condition=%wide.region_6.6_spmd, body=%wide.region_3.5_spmd.sunk | while | flops 206570016 | bytes 4627243 | solution.py:78
  396.9 2.9 fusion.43
  401.0 2.9 fusion.43
  405.0 8.3 %while.115 = (s32[]{:T(128)}, f32[32,256]{1,0:T(8,128)S(1)}, f32[32,256]{1,0:T(8,128)S(1)}, s32[]{:T(128)}, s32[24]{0:T(128)S(1)}, /*index=5*/s32[32]{0:T(128)S(...) while((s32[]{:T(128)}, f32[32,256]{1,0:T(8,128)S(1)}, ...), condition=%wide.region_11.11_spmd, body=%wide.region_7.10_spmd.sunk | while | flops 208300816 | bytes 4961095 | solution.py:112
  421.0 12.1 %while.114 = (s32[]{:T(128)}, f32[256]{0:T(256)S(1)}, f32[256]{0:T(256)S(1)}, s32[]{:T(128)}, s32[8]{0:T(128)S(1)}, /*index=5*/s32[]{:T(128)}, f32[24,35,256]{2,...) while((s32[]{:T(128)}, f32[256]{0:T(256)S(1)}, ...), condition=%wide.region_6.6_spmd, body=%wide.region_3.5_spmd.sunk | while | flops 206570016 | bytes 4627243 | solution.py:78
  421.8 2.9 fusion.43
  425.8 2.9 fusion.43
  429.8 2.9 fusion.43
  433.9 12.5 %while.115 = (s32[]{:T(128)}, f32[32,256]{1,0:T(8,128)S(1)}, f32[32,256]{1,0:T(8,128)S(1)}, s32[]{:T(128)}, s32[24]{0:T(128)S(1)}, /*index=5*/s32[32]{0:T(128)S(...) while((s32[]{:T(128)}, f32[32,256]{1,0:T(8,128)S(1)}, ...), condition=%wide.region_11.11_spmd, body=%wide.region_7.10_spmd.sunk | while | flops 208300816 | bytes 4961095 | solution.py:112
  454.0 12.1 %while.114 = (s32[]{:T(128)}, f32[256]{0:T(256)S(1)}, f32[256]{0:T(256)S(1)}, s32[]{:T(128)}, s32[8]{0:T(128)S(1)}, /*index=5*/s32[]{:T(128)}, f32[24,35,256]{2,...) while((s32[]{:T(128)}, f32[256]{0:T(256)S(1)}, ...), condition=%wide.region_6.6_spmd, body=%wide.region_3.5_spmd.sunk | while | flops 206570016 | bytes 4627243 | solution.py:78
  454.8 2.9 fusion.43
  462.9 2.9 fusion.43
  466.9 12.5 %while.115 = (s32[]{:T(128)}, f32[32,256]{1,0:T(8,128)S(1)}, f32[32,256]{1,0:T(8,128)S(1)}, s32[]{:T(128)}, s32[24]{0:T(128)S(1)}, /*index=5*/s32[32]{0:T(128)S(...) while((s32[]{:T(128)}, f32[32,256]{1,0:T(8,128)S(1)}, ...), condition=%wide.region_11.11_spmd, body=%wide.region_7.10_spmd.sunk | while | flops 208300816 | bytes 4961095 | solution.py:112
  487.0 8.1 %while.114 = (s32[]{:T(128)}, f32[256]{0:T(256)S(1)}, f32[256]{0:T(256)S(1)}, s32[]{:T(128)}, s32[8]{0:T(128)S(1)}, /*index=5*/s32[]{:T(128)}, f32[24,35,256]{2,...) while((s32[]{:T(128)}, f32[256]{0:T(256)S(1)}, ...), condition=%wide.region_6.6_spmd, body=%wide.region_3.5_spmd.sunk | while | flops 206570016 | bytes 4627243 | solution.py:78
  487.8 2.9 fusion.43
  495.9 8.3 %while.115 = (s32[]{:T(128)}, f32[32,256]{1,0:T(8,128)S(1)}, f32[32,256]{1,0:T(8,128)S(1)}, s32[]{:T(128)}, s32[24]{0:T(128)S(1)}, /*index=5*/s32[32]{0:T(128)S(...) while((s32[]{:T(128)}, f32[32,256]{1,0:T(8,128)S(1)}, ...), condition=%wide.region_11.11_spmd, body=%wide.region_7.10_spmd.sunk | while | flops 208300816 | bytes 4961095 | solution.py:112
  504.4 114.5 %all-gather.1 = f32[16,1,8192]{2,1,0:T(1,128)S(1)} all-gather(f32[1,1,8192]{2,1,0:T(1,128)S(1)} %reshape.237), channel_id=1, replica_groups=mesh['parts'=2,'rows'=2,'cols'=8] {'rows','cols'}, dimensions={0}, use_global_device_ids=true | all-gather | bytes 557056 | tf_op jit(solution)/shard_map/all_gather | solution.py:14
  619.2 31.4 %all-gather = f32[16,1,8192]{2,1,0:T(1,128)S(1)} all-gather(f32[1,1,8192]{2,1,0:T(1,128)S(1)} %reshape.235), channel_id=1, replica_groups=mesh['parts'=2,'rows'=2,'cols'=8] {'rows','cols'}, dimensions={0}, use_global_device_ids=true | all-gather | bytes 557056 | tf_op jit(solution)/shard_map/all_gather | solution.py:14
  (1066 shorter events, 316.6 us)
Async XLA Ops:
  7.2 47.8 %all-gather.4.cloned.1.call-start = ((), (), s32[]{:S(2)}) async-start(), calls=%async_computation | async-start | bytes 1474560 | tf_op jit(solution)/shard_map/all_gather | solution.py:32
  55.0 2.0 copy-start
  57.1 0.9 copy-start.1
Sparse Core Ops, SparseCore 0:
  10.2 44.7 all-gather.3
where the time goes:
time: 665 us; the launch traced here: 661 us
  matrix products  216 us (32%)
  blocking collectives  146 us (22%)
  other arithmetic  126 us (19%)
  loops' own time  59.5 us (9%)
  local copies, waits for them, and re-layouts  53.3 us (8%)
  waiting for transfers between devices  46.1 us (7%)
  between operations  14.2 us (2%)
    dot_general x76, matrix products, take_group(): jnp.einsum('dr,gdc->rgc', xs, group[:, :D, :], precision=lax.Precision.HI...  198 us
    all_gather x2, blocking collectives, joined(): everything = jax.tree.map(lambda part: lax.all_gather(part, axis), array)  146 us
    another operation x1, loops' own time, on_device(): lax.scan(row_step, init, jnp.arange(pairs.shape[0], dtype=jnp.int32))  53.5 us
    lt x76, other arithmetic, take_group(): mask = jnp.repeat(step * GROUP + within < count, BLK)  52.8 us
    all_gather x1, waiting for transfers between devices, on_device(): whole = lax.all_gather(packed, 'cols', axis=1, tiled=True)  46.1 us
    reduce_sum x38, other arithmetic, row_pass(): jnp.sum(jnp.exp(scores - top[:, None]), axis=1)  13.7 us
    select_n x32, other arithmetic, row_step(): slabs = jnp.take(blocks, row_ids, axis=0)  13.3 us
  transfers between devices with their start and end apart: 1, of which 1 were waited for; matrix products, arithmetic and copies ran while one was open for 0% of the time, Pallas kernels for 0%

commit v1 on v0

--- a/solution.py
+++ b/solution.py
@@ -29,7 +29,23 @@
 def on_device(src_feat, tgt_feat, tgt_pot, log_src, log_tgt, pairs, counts):
     own_targets = tgt_feat.shape[1]
     packed = jnp.concatenate([tgt_feat, tgt_pot[None, :], log_tgt[None, :]], axis=0)
-    whole = lax.all_gather(packed, "cols", axis=1, tiled=True)
+    size, mine, extent = (lax.axis_size("cols"), lax.axis_index("cols"), packed.shape[1])
+    upward = [(i, (i + 1) % size) for i in range(size)]
+    left = [(i, (i - 1) % size) for i in range(size)]
+    whole = jnp.zeros((*packed.shape[:1], size * extent, *packed.shape[1 + 1 :]), packed.dtype)
+    whole = lax.dynamic_update_slice_in_dim(whole, packed, mine * extent, axis=1)
+    from_left = from_right = packed
+    half = size // 2
+    for step_2 in range(1, half + 1):
+        from_left = lax.ppermute(from_left, "cols", upward)
+        whole = lax.dynamic_update_slice_in_dim(
+            whole, from_left, (mine - step_2) % size * extent, axis=1
+        )
+        if step_2 < size - half:
+            from_right = lax.ppermute(from_right, "cols", left)
+            whole = lax.dynamic_update_slice_in_dim(
+                whole, from_right, (mine + step_2) % size * extent, axis=1
+            )
     feats = whole[:D]
     ynorm = jnp.sum(feats * feats, axis=0)
     tblocks = whole.shape[1] // BLK

time: 665 us -> 625 us (0.940)
  waiting for transfers between devices: 46.1 us -> 19.5 us
  starting transfers between devices: 0.04 us -> 19.5 us
  between operations: 14.2 us -> 0.84 us
  other arithmetic: 126 us -> 115 us
    all_gather x1 -> x0, waiting for transfers between devices: 46.1 us -> none  [on_device(): whole = lax.all_gather(packed, 'cols', axis=1, tiled=True)]
    ppermute x0 -> x7, waiting for transfers between devices: none -> 19.5 us  [the longest x4 19.5 us: on_device(): from_left = lax.ppermute(from_left, 'cols', upward)]
    ppermute x0 -> x7, starting transfers between devices: none -> 19.5 us  [the longest x3 10.7 us: on_device(): from_right = lax.ppermute(from_right, 'cols', left)]
    lt x76, other arithmetic: 52.8 us -> 42.9 us  [take_group(): mask = jnp.repeat(step * GROUP + within < count, BLK)]
  transfers between devices with their start and end apart: 1 -> 7, of which waited for: 1 -> 4; matrix products, arithmetic and copies ran while one was open for 0% -> 0% of each run, Pallas kernels for 0% -> 0%
where the time goes in v1:
time: 625 us; the launch traced here: 621 us
  matrix products  216 us (35%)
  blocking collectives  141 us (23%)
  other arithmetic  115 us (18%)
  loops' own time  57.2 us (9%)
  local copies, waits for them, and re-layouts  51.2 us (8%)
  starting transfers between devices  19.5 us (3%)
  waiting for transfers between devices  19.5 us (3%)
    dot_general x76, matrix products, take_group(): jnp.einsum('dr,gdc->rgc', xs, group[:, :D, :], precision=lax.Precision.HI...  198 us
    all_gather x2, blocking collectives, joined(): everything = jax.tree.map(lambda part: lax.all_gather(part, axis), array)  141 us
    another operation x1, loops' own time, on_device(): lax.scan(row_step, init, jnp.arange(pairs.shape[0], dtype=jnp.int32))  51.3 us
    lt x76, other arithmetic, take_group(): mask = jnp.repeat(step * GROUP + within < count, BLK)  42.9 us
    ppermute x4, waiting for transfers between devices, on_device(): from_left = lax.ppermute(from_left, 'cols', upward)  19.5 us
    reduce_sum x38, other arithmetic, row_pass(): jnp.sum(jnp.exp(scores - top[:, None]), axis=1)  13.7 us
    select_n x32, other arithmetic, row_step(): slabs = jnp.take(blocks, row_ids, axis=0)  13.3 us
    reduce_sum x16, other arithmetic, row_step(): xnorm = jnp.sum(xs * xs, axis=0)  12.5 us
  transfers between devices with their start and end apart: 7, of which 4 were waited for; matrix products, arithmetic and copies ran while one was open for 0% of the time, Pallas kernels for 0%

profile of v1, /device:TPU:0, one launch (start us, length us, event | category | flops | bytes accessed | tf_op | source)
XLA Modules:
  0.0 620.8 jit_solution(15962627419167027179)
XLA Ops:
  1.7 3.0 collective-permute-start
  4.7 3.1 collective-permute-start.1
  7.8 4.2 collective-permute-done
  14.2 3.6 collective-permute-start.3
  17.8 4.1 collective-permute-done.2
  24.4 3.9 collective-permute-start.5
  28.4 4.5 collective-permute-done.4
  34.2 6.7 %collective-permute-done.6 = f32[34,1024]{1,0:T(8,128)S(1)} collective-permute-done((f32[34,1024]{1,0:T(8,128)S(1)}, f32[34,1024]{1,0:T(8,128)S(1)}, u32[]{:S(2)}, u32[]{:S(2)}) %collective-permute-start.6) | collective-permute-done | bytes 139296 | tf_op jit(solution)/shard_map/ppermute | solution.py:40
  42.5 433.4 %while.113 = (s32[]{:T(128)}, f32[32,256]{1,0:T(8,128)S(1)}, f32[32,256]{1,0:T(8,128)S(1)}, f32[16,256]{1,0:T(8,128)S(1)}, s32[16]{0:T(128)S(1)}, /*index=5*/s32...) while((s32[]{:T(128)}, f32[32,256]{1,0:T(8,128)S(1)}, ...), condition=%wide.region_12.13_spmd.clone.clone, body=%wide.region_1.12_spmd.clone.clone.sunk | while | flops 415103776 | bytes 13110493 | solution.py:132
  49.8 11.8 %while.114 = (s32[]{:T(128)}, f32[256]{0:T(256)S(1)}, f32[256]{0:T(256)S(1)}, s32[]{:T(128)}, s32[8]{0:T(128)S(1)}, /*index=5*/s32[]{:T(128)}, f32[24,35,256]{2,...) while((s32[]{:T(128)}, f32[256]{0:T(256)S(1)}, ...), condition=%wide.region_6.6_spmd, body=%wide.region_3.5_spmd.sunk | while | flops 206570016 | bytes 4627243 | solution.py:94
  50.5 2.9 fusion.43
  54.4 2.9 fusion.43
  58.3 2.9 fusion.43
  62.4 12.1 %while.115 = (s32[]{:T(128)}, f32[32,256]{1,0:T(8,128)S(1)}, f32[32,256]{1,0:T(8,128)S(1)}, s32[]{:T(128)}, s32[24]{0:T(128)S(1)}, /*index=5*/s32[32]{0:T(128)S(...) while((s32[]{:T(128)}, f32[32,256]{1,0:T(8,128)S(1)}, ...), condition=%wide.region_11.11_spmd, body=%wide.region_7.10_spmd.sunk | while | flops 208300816 | bytes 4961095 | solution.py:128
  81.9 3.9 while.114
  82.5 2.9 fusion.43
  86.6 4.0 while.115
  98.0 11.8 %while.114 = (s32[]{:T(128)}, f32[256]{0:T(256)S(1)}, f32[256]{0:T(256)S(1)}, s32[]{:T(128)}, s32[8]{0:T(128)S(1)}, /*index=5*/s32[]{:T(128)}, f32[24,35,256]{2,...) while((s32[]{:T(128)}, f32[256]{0:T(256)S(1)}, ...), condition=%wide.region_6.6_spmd, body=%wide.region_3.5_spmd.sunk | while | flops 206570016 | bytes 4627243 | solution.py:94
  98.7 2.9 fusion.43
  102.6 2.9 fusion.43
  106.5 2.9 fusion.43
  110.6 12.1 %while.115 = (s32[]{:T(128)}, f32[32,256]{1,0:T(8,128)S(1)}, f32[32,256]{1,0:T(8,128)S(1)}, s32[]{:T(128)}, s32[24]{0:T(128)S(1)}, /*index=5*/s32[32]{0:T(128)S(...) while((s32[]{:T(128)}, f32[32,256]{1,0:T(8,128)S(1)}, ...), condition=%wide.region_11.11_spmd, body=%wide.region_7.10_spmd.sunk | while | flops 208300816 | bytes 4961095 | solution.py:128
  130.1 7.8 %while.114 = (s32[]{:T(128)}, f32[256]{0:T(256)S(1)}, f32[256]{0:T(256)S(1)}, s32[]{:T(128)}, s32[8]{0:T(128)S(1)}, /*index=5*/s32[]{:T(128)}, f32[24,35,256]{2,...) while((s32[]{:T(128)}, f32[256]{0:T(256)S(1)}, ...), condition=%wide.region_6.6_spmd, body=%wide.region_3.5_spmd.sunk | while | flops 206570016 | bytes 4627243 | solution.py:94
  130.7 2.9 fusion.43
  134.7 2.9 fusion.43
  138.7 8.1 %while.115 = (s32[]{:T(128)}, f32[32,256]{1,0:T(8,128)S(1)}, f32[32,256]{1,0:T(8,128)S(1)}, s32[]{:T(128)}, s32[24]{0:T(128)S(1)}, /*index=5*/s32[32]{0:T(128)S(...) while((s32[]{:T(128)}, f32[32,256]{1,0:T(8,128)S(1)}, ...), condition=%wide.region_11.11_spmd, body=%wide.region_7.10_spmd.sunk | while | flops 208300816 | bytes 4961095 | solution.py:128
  154.2 11.8 %while.114 = (s32[]{:T(128)}, f32[256]{0:T(256)S(1)}, f32[256]{0:T(256)S(1)}, s32[]{:T(128)}, s32[8]{0:T(128)S(1)}, /*index=5*/s32[]{:T(128)}, f32[24,35,256]{2,...) while((s32[]{:T(128)}, f32[256]{0:T(256)S(1)}, ...), condition=%wide.region_6.6_spmd, body=%wide.region_3.5_spmd.sunk | while | flops 206570016 | bytes 4627243 | solution.py:94
  154.8 2.9 fusion.43
  158.8 2.9 fusion.43
  162.7 2.9 fusion.43
  166.7 12.1 %while.115 = (s32[]{:T(128)}, f32[32,256]{1,0:T(8,128)S(1)}, f32[32,256]{1,0:T(8,128)S(1)}, s32[]{:T(128)}, s32[24]{0:T(128)S(1)}, /*index=5*/s32[32]{0:T(128)S(...) while((s32[]{:T(128)}, f32[32,256]{1,0:T(8,128)S(1)}, ...), condition=%wide.region_11.11_spmd, body=%wide.region_7.10_spmd.sunk | while | flops 208300816 | bytes 4961095 | solution.py:128
  186.3 11.8 %while.114 = (s32[]{:T(128)}, f32[256]{0:T(256)S(1)}, f32[256]{0:T(256)S(1)}, s32[]{:T(128)}, s32[8]{0:T(128)S(1)}, /*index=5*/s32[]{:T(128)}, f32[24,35,256]{2,...) while((s32[]{:T(128)}, f32[256]{0:T(256)S(1)}, ...), condition=%wide.region_6.6_spmd, body=%wide.region_3.5_spmd.sunk | while | flops 206570016 | bytes 4627243 | solution.py:94
  186.9 2.9 fusion.43
  190.8 2.9 fusion.43
  194.7 2.9 fusion.43
  198.8 12.1 %while.115 = (s32[]{:T(128)}, f32[32,256]{1,0:T(8,128)S(1)}, f32[32,256]{1,0:T(8,128)S(1)}, s32[]{:T(128)}, s32[24]{0:T(128)S(1)}, /*index=5*/s32[32]{0:T(128)S(...) while((s32[]{:T(128)}, f32[32,256]{1,0:T(8,128)S(1)}, ...), condition=%wide.region_11.11_spmd, body=%wide.region_7.10_spmd.sunk | while | flops 208300816 | bytes 4961095 | solution.py:128
  218.3 7.8 %while.114 = (s32[]{:T(128)}, f32[256]{0:T(256)S(1)}, f32[256]{0:T(256)S(1)}, s32[]{:T(128)}, s32[8]{0:T(128)S(1)}, /*index=5*/s32[]{:T(128)}, f32[24,35,256]{2,...) while((s32[]{:T(128)}, f32[256]{0:T(256)S(1)}, ...), condition=%wide.region_6.6_spmd, body=%wide.region_3.5_spmd.sunk | while | flops 206570016 | bytes 4627243 | solution.py:94
  219.0 2.9 fusion.43
  227.0 8.1 %while.115 = (s32[]{:T(128)}, f32[32,256]{1,0:T(8,128)S(1)}, f32[32,256]{1,0:T(8,128)S(1)}, s32[]{:T(128)}, s32[24]{0:T(128)S(1)}, /*index=5*/s32[32]{0:T(128)S(...) while((s32[]{:T(128)}, f32[32,256]{1,0:T(8,128)S(1)}, ...), condition=%wide.region_11.11_spmd, body=%wide.region_7.10_spmd.sunk | while | flops 208300816 | bytes 4961095 | solution.py:128
  242.4 11.8 %while.114 = (s32[]{:T(128)}, f32[256]{0:T(256)S(1)}, f32[256]{0:T(256)S(1)}, s32[]{:T(128)}, s32[8]{0:T(128)S(1)}, /*index=5*/s32[]{:T(128)}, f32[24,35,256]{2,...) while((s32[]{:T(128)}, f32[256]{0:T(256)S(1)}, ...), condition=%wide.region_6.6_spmd, body=%wide.region_3.5_spmd.sunk | while | flops 206570016 | bytes 4627243 | solution.py:94
  255.0 12.1 %while.115 = (s32[]{:T(128)}, f32[32,256]{1,0:T(8,128)S(1)}, f32[32,256]{1,0:T(8,128)S(1)}, s32[]{:T(128)}, s32[24]{0:T(128)S(1)}, /*index=5*/s32[32]{0:T(128)S(...) while((s32[]{:T(128)}, f32[32,256]{1,0:T(8,128)S(1)}, ...), condition=%wide.region_11.11_spmd, body=%wide.region_7.10_spmd.sunk | while | flops 208300816 | bytes 4961095 | solution.py:128
  274.5 7.8 %while.114 = (s32[]{:T(128)}, f32[256]{0:T(256)S(1)}, f32[256]{0:T(256)S(1)}, s32[]{:T(128)}, s32[8]{0:T(128)S(1)}, /*index=5*/s32[]{:T(128)}, f32[24,35,256]{2,...) while((s32[]{:T(128)}, f32[256]{0:T(256)S(1)}, ...), condition=%wide.region_6.6_spmd, body=%wide.region_3.5_spmd.sunk | while | flops 206570016 | bytes 4627243 | solution.py:94
  279.1 2.9 fusion.43
  283.1 8.1 %while.115 = (s32[]{:T(128)}, f32[32,256]{1,0:T(8,128)S(1)}, f32[32,256]{1,0:T(8,128)S(1)}, s32[]{:T(128)}, s32[24]{0:T(128)S(1)}, /*index=5*/s32[32]{0:T(128)S(...) while((s32[]{:T(128)}, f32[32,256]{1,0:T(8,128)S(1)}, ...), condition=%wide.region_11.11_spmd, body=%wide.region_7.10_spmd.sunk | while | flops 208300816 | bytes 4961095 | solution.py:128
  298.6 7.8 %while.114 = (s32[]{:T(128)}, f32[256]{0:T(256)S(1)}, f32[256]{0:T(256)S(1)}, s32[]{:T(128)}, s32[8]{0:T(128)S(1)}, /*index=5*/s32[]{:T(128)}, f32[24,35,256]{2,...) while((s32[]{:T(128)}, f32[256]{0:T(256)S(1)}, ...), condition=%wide.region_6.6_spmd, body=%wide.region_3.5_spmd.sunk | while | flops 206570016 | bytes 4627243 | solution.py:94
  307.2 8.1 %while.115 = (s32[]{:T(128)}, f32[32,256]{1,0:T(8,128)S(1)}, f32[32,256]{1,0:T(8,128)S(1)}, s32[]{:T(128)}, s32[24]{0:T(128)S(1)}, /*index=5*/s32[32]{0:T(128)S(...) while((s32[]{:T(128)}, f32[32,256]{1,0:T(8,128)S(1)}, ...), condition=%wide.region_11.11_spmd, body=%wide.region_7.10_spmd.sunk | while | flops 208300816 | bytes 4961095 | solution.py:128
  322.7 7.8 %while.114 = (s32[]{:T(128)}, f32[256]{0:T(256)S(1)}, f32[256]{0:T(256)S(1)}, s32[]{:T(128)}, s32[8]{0:T(128)S(1)}, /*index=5*/s32[]{:T(128)}, f32[24,35,256]{2,...) while((s32[]{:T(128)}, f32[256]{0:T(256)S(1)}, ...), condition=%wide.region_6.6_spmd, body=%wide.region_3.5_spmd.sunk | while | flops 206570016 | bytes 4627243 | solution.py:94
  323.4 2.9 fusion.43
  331.3 8.1 %while.115 = (s32[]{:T(128)}, f32[32,256]{1,0:T(8,128)S(1)}, f32[32,256]{1,0:T(8,128)S(1)}, s32[]{:T(128)}, s32[24]{0:T(128)S(1)}, /*index=5*/s32[32]{0:T(128)S(...) while((s32[]{:T(128)}, f32[32,256]{1,0:T(8,128)S(1)}, ...), condition=%wide.region_11.11_spmd, body=%wide.region_7.10_spmd.sunk | while | flops 208300816 | bytes 4961095 | solution.py:128
  346.8 7.8 %while.114 = (s32[]{:T(128)}, f32[256]{0:T(256)S(1)}, f32[256]{0:T(256)S(1)}, s32[]{:T(128)}, s32[8]{0:T(128)S(1)}, /*index=5*/s32[]{:T(128)}, f32[24,35,256]{2,...) while((s32[]{:T(128)}, f32[256]{0:T(256)S(1)}, ...), condition=%wide.region_6.6_spmd, body=%wide.region_3.5_spmd.sunk | while | flops 206570016 | bytes 4627243 | solution.py:94
  347.5 2.9 fusion.43
  355.4 8.1 %while.115 = (s32[]{:T(128)}, f32[32,256]{1,0:T(8,128)S(1)}, f32[32,256]{1,0:T(8,128)S(1)}, s32[]{:T(128)}, s32[24]{0:T(128)S(1)}, /*index=5*/s32[32]{0:T(128)S(...) while((s32[]{:T(128)}, f32[32,256]{1,0:T(8,128)S(1)}, ...), condition=%wide.region_11.11_spmd, body=%wide.region_7.10_spmd.sunk | while | flops 208300816 | bytes 4961095 | solution.py:128
  370.9 7.8 %while.114 = (s32[]{:T(128)}, f32[256]{0:T(256)S(1)}, f32[256]{0:T(256)S(1)}, s32[]{:T(128)}, s32[8]{0:T(128)S(1)}, /*index=5*/s32[]{:T(128)}, f32[24,35,256]{2,...) while((s32[]{:T(128)}, f32[256]{0:T(256)S(1)}, ...), condition=%wide.region_6.6_spmd, body=%wide.region_3.5_spmd.sunk | while | flops 206570016 | bytes 4627243 | solution.py:94
  379.5 8.1 %while.115 = (s32[]{:T(128)}, f32[32,256]{1,0:T(8,128)S(1)}, f32[32,256]{1,0:T(8,128)S(1)}, s32[]{:T(128)}, s32[24]{0:T(128)S(1)}, /*index=5*/s32[32]{0:T(128)S(...) while((s32[]{:T(128)}, f32[32,256]{1,0:T(8,128)S(1)}, ...), condition=%wide.region_11.11_spmd, body=%wide.region_7.10_spmd.sunk | while | flops 208300816 | bytes 4961095 | solution.py:128
  395.0 11.8 %while.114 = (s32[]{:T(128)}, f32[256]{0:T(256)S(1)}, f32[256]{0:T(256)S(1)}, s32[]{:T(128)}, s32[8]{0:T(128)S(1)}, /*index=5*/s32[]{:T(128)}, f32[24,35,256]{2,...) while((s32[]{:T(128)}, f32[256]{0:T(256)S(1)}, ...), condition=%wide.region_6.6_spmd, body=%wide.region_3.5_spmd.sunk | while | flops 206570016 | bytes 4627243 | solution.py:94
  407.5 12.1 %while.115 = (s32[]{:T(128)}, f32[32,256]{1,0:T(8,128)S(1)}, f32[32,256]{1,0:T(8,128)S(1)}, s32[]{:T(128)}, s32[24]{0:T(128)S(1)}, /*index=5*/s32[32]{0:T(128)S(...) while((s32[]{:T(128)}, f32[32,256]{1,0:T(8,128)S(1)}, ...), condition=%wide.region_11.11_spmd, body=%wide.region_7.10_spmd.sunk | while | flops 208300816 | bytes 4961095 | solution.py:128
  427.1 11.8 %while.114 = (s32[]{:T(128)}, f32[256]{0:T(256)S(1)}, f32[256]{0:T(256)S(1)}, s32[]{:T(128)}, s32[8]{0:T(128)S(1)}, /*index=5*/s32[]{:T(128)}, f32[24,35,256]{2,...) while((s32[]{:T(128)}, f32[256]{0:T(256)S(1)}, ...), condition=%wide.region_6.6_spmd, body=%wide.region_3.5_spmd.sunk | while | flops 206570016 | bytes 4627243 | solution.py:94
  427.7 2.9 fusion.43
  435.6 2.9 fusion.43
  439.6 12.1 %while.115 = (s32[]{:T(128)}, f32[32,256]{1,0:T(8,128)S(1)}, f32[32,256]{1,0:T(8,128)S(1)}, s32[]{:T(128)}, s32[24]{0:T(128)S(1)}, /*index=5*/s32[32]{0:T(128)S(...) while((s32[]{:T(128)}, f32[32,256]{1,0:T(8,128)S(1)}, ...), condition=%wide.region_11.11_spmd, body=%wide.region_7.10_spmd.sunk | while | flops 208300816 | bytes 4961095 | solution.py:128
  459.1 7.8 %while.114 = (s32[]{:T(128)}, f32[256]{0:T(256)S(1)}, f32[256]{0:T(256)S(1)}, s32[]{:T(128)}, s32[8]{0:T(128)S(1)}, /*index=5*/s32[]{:T(128)}, f32[24,35,256]{2,...) while((s32[]{:T(128)}, f32[256]{0:T(256)S(1)}, ...), condition=%wide.region_6.6_spmd, body=%wide.region_3.5_spmd.sunk | while | flops 206570016 | bytes 4627243 | solution.py:94
  467.8 8.1 %while.115 = (s32[]{:T(128)}, f32[32,256]{1,0:T(8,128)S(1)}, f32[32,256]{1,0:T(8,128)S(1)}, s32[]{:T(128)}, s32[24]{0:T(128)S(1)}, /*index=5*/s32[32]{0:T(128)S(...) while((s32[]{:T(128)}, f32[32,256]{1,0:T(8,128)S(1)}, ...), condition=%wide.region_11.11_spmd, body=%wide.region_7.10_spmd.sunk | while | flops 208300816 | bytes 4961095 | solution.py:128
  475.9 109.6 %all-gather.1 = f32[16,1,8192]{2,1,0:T(1,128)S(1)} all-gather(f32[1,1,8192]{2,1,0:T(1,128)S(1)} %reshape.237), channel_id=1, replica_groups=mesh['parts'=2,'rows'=2,'cols'=8] {'rows','cols'}, dimensions={0}, use_global_device_ids=true | all-gather | bytes 557056 | tf_op jit(solution)/shard_map/all_gather | solution.py:14
  585.9 31.6 %all-gather = f32[16,1,8192]{2,1,0:T(1,128)S(1)} all-gather(f32[1,1,8192]{2,1,0:T(1,128)S(1)} %reshape.235), channel_id=1, replica_groups=mesh['parts'=2,'rows'=2,'cols'=8] {'rows','cols'}, dimensions={0}, use_global_device_ids=true | all-gather | bytes 557056 | tf_op jit(solution)/shard_map/all_gather | solution.py:14
  (1083 shorter events, 329.9 us)
Async XLA Ops:
  1.7 10.4 %collective-permute-start = (f32[34,1024]{1,0:T(8,128)S(1)}, f32[34,1024]{1,0:T(8,128)S(1)}, u32[]{:S(2)}, u32[]{:S(2)}) collective-permute-start(f32[34,1024]{1,0:T(8,128)S(1)} %get-tuple-element.724), channel_id=1, source_target_pairs={{0,1},{1,2},{2,3},{3,4},{4,5},{5,6},{6,7},{7,0},{8,9},{9,10},{10,1... | collective-permute-start | bytes 417800 | tf_op jit(solution)/shard_map/ppermute | solution.py:40
  4.7 9.5 %collective-permute-start.1 = (f32[34,1024]{1,0:T(8,128)S(1)}, f32[34,1024]{1,0:T(8,128)S(1)}, u32[]{:S(2)}, u32[]{:S(2)}) collective-permute-start(f32[34,1024]{1,0:T(8,128)S(1)} %get-tuple-element.724), channel_id=1, source_target_pairs={{0,7},{1,0},{2,1},{3,2},{4,3},{5,4},{6,5},{7,6},{8,15},{9,8},{10,9... | collective-permute-start | bytes 417800 | tf_op jit(solution)/shard_map/ppermute | solution.py:45
  12.1 9.9 %collective-permute-start.2 = (f32[34,1024]{1,0:T(8,128)S(1)}, f32[34,1024]{1,0:T(8,128)S(1)}, u32[]{:S(2)}, u32[]{:S(2)}) collective-permute-start(f32[34,1024]{1,0:T(8,128)S(1)} %collective-permute-done), channel_id=1, source_target_pairs={{0,1},{1,2},{2,3},{3,4},{4,5},{5,6},{6,7},{7,0},{8,9},{9,10},{10,1... | collective-permute-start | bytes 417800 | tf_op jit(solution)/shard_map/ppermute | solution.py:40
  14.2 10.2 %collective-permute-start.3 = (f32[34,1024]{1,0:T(8,128)S(1)}, f32[34,1024]{1,0:T(8,128)S(1)}, u32[]{:S(2)}, u32[]{:S(2)}) collective-permute-start(f32[34,1024]{1,0:T(8,128)S(1)} %collective-permute-done.1), channel_id=1, source_target_pairs={{0,7},{1,0},{2,1},{3,2},{4,3},{5,4},{6,5},{7,6},{8,15},{9,8},{10,9... | collective-permute-start | bytes 417800 | tf_op jit(solution)/shard_map/ppermute | solution.py:45
  21.9 10.9 %collective-permute-start.4 = (f32[34,1024]{1,0:T(8,128)S(1)}, f32[34,1024]{1,0:T(8,128)S(1)}, u32[]{:S(2)}, u32[]{:S(2)}) collective-permute-start(f32[34,1024]{1,0:T(8,128)S(1)} %collective-permute-done.2), channel_id=1, source_target_pairs={{0,1},{1,2},{2,3},{3,4},{4,5},{5,6},{6,7},{7,0},{8,9},{9,10},{10,1... | collective-permute-start | bytes 417800 | tf_op jit(solution)/shard_map/ppermute | solution.py:40
  24.4 9.7 %collective-permute-start.5 = (f32[34,1024]{1,0:T(8,128)S(1)}, f32[34,1024]{1,0:T(8,128)S(1)}, u32[]{:S(2)}, u32[]{:S(2)}) collective-permute-start(f32[34,1024]{1,0:T(8,128)S(1)} %collective-permute-done.3), channel_id=1, source_target_pairs={{0,7},{1,0},{2,1},{3,2},{4,3},{5,4},{6,5},{7,6},{8,15},{9,8},{10,9... | collective-permute-start | bytes 417800 | tf_op jit(solution)/shard_map/ppermute | solution.py:45
  32.9 8.0 %collective-permute-start.6 = (f32[34,1024]{1,0:T(8,128)S(1)}, f32[34,1024]{1,0:T(8,128)S(1)}, u32[]{:S(2)}, u32[]{:S(2)}) collective-permute-start(f32[34,1024]{1,0:T(8,128)S(1)} %collective-permute-done.4), channel_id=1, source_target_pairs={{0,1},{1,2},{2,3},{3,4},{4,5},{5,6},{6,7},{7,0},{8,9},{9,10},{10,1... | collective-permute-start | bytes 417800 | tf_op jit(solution)/shard_map/ppermute | solution.py:40
  41.6 0.9 copy-start
